TPU v7x, 128 devices: a whole 4x4x4 slice. The times are simulated.
128 devices in a mesh: leaf: 4 (over x), blk: 32 (over y, z, core).
Axes of the slice: x: 4, y: 4, z: 4, core: 2. Of those that a mesh axis runs over, the one named last changes fastest.
Arguments:
- diag_blocks: float32 [4, 512, 512], P('leaf'), as said below
- panel: float32 [4, 128, 256, 512], P('leaf', 'blk'), may hold values from -1.2 to 1.2
- local_targets: bfloat16 [4, 2560, 256, 256], P('leaf', 'blk'), may hold values from -6 to 6
- local_pairs: int32 [4, 2560, 2], P('leaf', 'blk'), may hold values from -1 to 127, as said below
- top_targets: bfloat16 [32, 16, 256, 256], P('blk', 'leaf'), may hold values from -6 to 6
- top_pairs: int32 [32, 16, 2], P('blk'), may hold values from 0 to 255
- top_pattern: int32 [4, 256], P('leaf'), may hold values from -1 to 127, as said below
Outputs:
- panel_factor: bfloat16 [4, 128, 256, 512], P('leaf', 'blk')
- local_updated: bfloat16 [4, 2560, 256, 256], P('leaf', 'blk')
- top_updated: bfloat16 [32, 16, 256, 256], P('blk', 'leaf')
Inputs may be any that keep to these rules, and one draw needn't show every extreme that they name: Each diag_blocks[g] is symmetric positive definite with smallest eigenvalue 0.5 or more. `local_pairs`: empty slots hold -1 in both columns; on each device the live slots come first; some device has all 80 slots live. `top_pattern`: in each group every panel row 0 to 127 stands at exactly one ancestor row; the other ancestor rows hold -1.
All inputs are finite; a program needn't handle non-finite values.
Results may differ from a plain program's by a relative error of at most 0.014.
Values may be sent and summed in bfloat16 or wider, within the bound.
No kernel may reach another device: no remote copies, remote signals or barrier semaphores. Data moves between devices by JAX's collectives and lax.ppermute only.
A program may use at most 192 MiB of HBM per device.

v0:
```python
import functools

import jax
import jax.numpy as jnp
from jax import lax
from jax.experimental import pallas as pl
from jax.experimental.pallas import tpu as pltpu
from jax.sharding import PartitionSpec as P


def _pair_kernel(k, has_targets, left_ref, right_ref, live_ref, *refs):
    lrefs = refs[:k]
    rrefs = refs[k:2 * k]
    out_ref = refs[-1]
    step = pl.program_id(0)
    for j in range(k):
        live = live_ref[step * k + j] > 0

        def product(j=j):
            return lax.dot_general(
                lrefs[j][0], rrefs[j][0], (((1,), (1,)), ((), ())),
                preferred_element_type=jnp.float32,
            )

        if has_targets:
            t_ref = refs[2 * k]

            @pl.when(live)
            def _(j=j):
                out_ref[j] = (t_ref[j].astype(jnp.float32) - product()).astype(out_ref.dtype)

            @pl.when(jnp.logical_not(live))
            def _(j=j):
                out_ref[j] = t_ref[j]
        else:

            @pl.when(live)
            def _(j=j):
                out_ref[j] = product().astype(out_ref.dtype)

            @pl.when(jnp.logical_not(live))
            def _(j=j):
                out_ref[j] = jnp.zeros(out_ref.shape[1:], out_ref.dtype)


def pair_products(rows_all, left, right, live, targets, k):
    count = left.shape[0]
    _, width, depth = rows_all.shape
    steps = count // k

    def row_map(j, which):
        def index(i, l_ref, r_ref, v_ref):
            ref = l_ref if which == 0 else r_ref
            return (ref[i * k + j], 0, 0)

        return index

    in_specs = [pl.BlockSpec((1, width, depth), row_map(j, 0)) for j in range(k)]
    in_specs += [pl.BlockSpec((1, width, depth), row_map(j, 1)) for j in range(k)]
    operands = [rows_all] * (2 * k)
    block_map = lambda i, l_ref, r_ref, v_ref: (i, 0, 0)
    if targets is not None:
        in_specs.append(pl.BlockSpec((k, width, width), block_map))
        operands.append(targets)
    grid_spec = pltpu.PrefetchScalarGridSpec(
        num_scalar_prefetch=3,
        grid=(steps,),
        in_specs=in_specs,
        out_specs=pl.BlockSpec((k, width, width), block_map),
    )
    flops = 2 * count * width * width * depth
    bytes_accessed = count * (2 * width * depth * 2 + 2 * width * width * 2)
    return pl.pallas_call(
        functools.partial(_pair_kernel, k, targets is not None),
        grid_spec=grid_spec,
        out_shape=jax.ShapeDtypeStruct((count, width, width), jnp.bfloat16),
        compiler_params=pltpu.CompilerParams(dimension_semantics=("arbitrary",)),
        cost_estimate=pl.CostEstimate(flops=flops, bytes_accessed=bytes_accessed, transcendentals=0),
    )(left, right, live, *operands)


def _step_of(count, limit=4):
    for k in range(limit, 0, -1):
        if count % k == 0:
            return k
    return 1

def _dot(a, b):
    return jnp.dot(a, b, precision=lax.Precision.HIGHEST)


def _inverse_factor(matrix, block):
    order = matrix.shape[0]
    nb = order // block
    eye = jnp.eye(block, dtype=matrix.dtype)
    trailing = matrix
    factor = {}
    diag_inv = []
    for k in range(nb):
        head = trailing[:block, :block]
        l_kk = jnp.linalg.cholesky(head)
        inv_kk = jax.scipy.linalg.solve_triangular(l_kk, eye, lower=True)
        diag_inv.append(inv_kk)
        if k + 1 < nb:
            below = _dot(trailing[block:, :block], inv_kk.T)
            for i in range(k + 1, nb):
                factor[(i, k)] = below[(i - k - 1) * block:(i - k) * block]
            trailing = trailing[block:, block:] - _dot(below, below.T)

    def inverse_of(lo, hi):
        if hi - lo == 1:
            return diag_inv[lo]
        mid = (lo + hi) // 2
        upper = inverse_of(lo, mid)
        lower = inverse_of(mid, hi)
        coupling = jnp.concatenate(
            [jnp.concatenate([factor[(i, j)] for j in range(lo, mid)], axis=1) for i in range(mid, hi)],
            axis=0,
        )
        corner = -_dot(lower, _dot(coupling, upper))
        top = jnp.concatenate([upper, jnp.zeros((upper.shape[0], lower.shape[1]), upper.dtype)], axis=1)
        bottom = jnp.concatenate([corner, lower], axis=1)
        return jnp.concatenate([top, bottom], axis=0)

    return inverse_of(0, nb)


def on_device(diag_blocks, panel, local_targets, local_pairs, top_targets, top_pairs, top_pattern):
    diagonal = diag_blocks[0]
    order = diagonal.shape[0]
    rows_local = panel[0]
    count, width, depth = rows_local.shape
    inverse = _inverse_factor(diagonal, 128)
    flat = rows_local.reshape(count * width, depth)
    joined = jnp.dot(flat, inverse.T, precision=lax.Precision.HIGHEST)
    panel_here = joined.reshape(count, width, depth).astype(jnp.bfloat16)

    rows_all = lax.all_gather(panel_here, "blk", axis=0, tiled=True)

    def position(g):
        return g

    targets_here = local_targets[0]
    pairs_here = local_pairs[0]
    live = (pairs_here[:, 0] >= 0).astype(jnp.int32)
    left = position(jnp.maximum(pairs_here[:, 0], 0))
    right = position(jnp.maximum(pairs_here[:, 1], 0))
    slots = targets_here.shape[0]
    updated = pair_products(rows_all, left, right, live, targets_here, _step_of(slots, 8))

    pattern = top_pattern[0]
    pairs_column = top_pairs[0]
    left_pos = jnp.take(pattern, pairs_column[:, 0], mode="clip")
    right_pos = jnp.take(pattern, pairs_column[:, 1], mode="clip")
    present = ((left_pos >= 0) & (right_pos >= 0)).astype(jnp.int32)
    top_count = pairs_column.shape[0]
    partial = pair_products(
        rows_all,
        position(jnp.maximum(left_pos, 0)),
        position(jnp.maximum(right_pos, 0)),
        present,
        None,
        _step_of(top_count),
    )
    summed = lax.psum_scatter(partial, "leaf", scatter_dimension=0, tiled=True).astype(jnp.float32)
    top_out = (top_targets[0].astype(jnp.float32) - summed).astype(jnp.bfloat16)[None]
    return (panel_here[None], updated[None], top_out)


def solution(mesh):
    in_specs = (
        P("leaf", None, None),
        P("leaf", "blk", None, None),
        P("leaf", "blk", None, None),
        P("leaf", "blk", None),
        P("blk", "leaf", None, None),
        P("blk", None, None),
        P("leaf", None),
    )
    out_specs = (
        P("leaf", "blk", None, None),
        P("leaf", "blk", None, None),
        P("blk", "leaf", None, None),
    )
    return jax.shard_map(on_device, mesh=mesh, in_specs=in_specs, out_specs=out_specs, check_vma=False)
```

profile of v0, /device:TPU:33, one launch (start us, length us, event | category | flops | bytes accessed | tf_op | source)
XLA Modules:
  0.0 275.9 jit_solution(15117548936018898363)
XLA Ops:
  7.2 0.0 copy-start
  7.2 0.0 all-gather.2.cloned.1.call-start
  7.2 1.7 copy.38
  8.9 0.1 copy.39
  9.1 11.7 %cholesky.74 = f32[128,128]{1,0:T(8,128)S(1)} custom-call(f32[128,128]{1,0:T(8,128)S(1)} %fusion.53), custom_call_target="Cholesky" | custom-call | tf_op jit(solution)/shard_map/jit(cholesky)/cholesky | solution.py:101
  20.8 0.6 compare_reduce_fusion.3
  21.5 0.7 fusion.38
  22.1 9.8 %custom-call.8 = f32[1,128,128]{1,2,0:T(8,128)S(1)} custom-call(f32[1,128,128]{2,1,0:T(8,128)S(1)} %fusion.38), custom_call_target="InvertDiagBlocksLowerTriangular" | custom-call | tf_op jit(solution)/shard_map/jit(_solve_triangular)/triangular_solve | solution.py:102
  31.9 0.3 fusion.34
  32.2 0.3 fusion.26
  32.5 0.7 convolution_subtract_fusion
  33.2 0.0 copy-start.3
  33.2 0.8 copy-done.3
  34.1 0.1 copy.41
  34.2 0.9 fusion.51
  35.0 11.7 %cholesky.85 = f32[128,128]{1,0:T(8,128)S(1)} custom-call(f32[128,128]{1,0:T(8,128)S(1)} %fusion.51), custom_call_target="Cholesky" | custom-call | tf_op jit(solution)/shard_map/jit(cholesky)/cholesky | solution.py:101
  46.8 0.6 compare_reduce_fusion.2
  47.4 0.7 fusion.39
  48.1 9.9 %custom-call.9 = f32[1,128,128]{1,2,0:T(8,128)S(1)} custom-call(f32[1,128,128]{2,1,0:T(8,128)S(1)} %fusion.39), custom_call_target="InvertDiagBlocksLowerTriangular" | custom-call | tf_op jit(solution)/shard_map/jit(_solve_triangular)/triangular_solve | solution.py:102
  58.0 0.3 fusion.32
  58.3 0.1 copy.43
  58.4 1.2 fusion.36
  59.6 0.3 fusion.44
  59.9 1.4 convolution_subtract_fusion.1
  61.3 0.1 copy.45
  61.4 11.7 %cholesky.96 = f32[128,128]{1,0:T(8,128)S(1)} custom-call(f32[128,128]{1,0:T(8,128)S(1)} %fusion.49), custom_call_target="Cholesky" | custom-call | tf_op jit(solution)/shard_map/jit(cholesky)/cholesky | solution.py:101
  73.2 0.6 compare_reduce_fusion.1
  73.8 0.7 fusion.40
  74.5 9.8 %custom-call.10 = f32[1,128,128]{1,2,0:T(8,128)S(1)} custom-call(f32[1,128,128]{2,1,0:T(8,128)S(1)} %fusion.40), custom_call_target="InvertDiagBlocksLowerTriangular" | custom-call | tf_op jit(solution)/shard_map/jit(_solve_triangular)/triangular_solve | solution.py:102
  84.3 0.3 fusion.30
  84.6 0.3 fusion.42
  84.9 0.3 convolution_subtract_fusion.2
  85.1 0.2 fusion.62
  85.4 0.3 convolution_negate_fusion.2
  85.7 0.1 copy.47
  85.8 11.9 %cholesky.107 = f32[128,128]{1,0:T(8,128)S(1)} custom-call(f32[128,128]{1,0:T(8,128)S(1)} %fusion.47), custom_call_target="Cholesky" | custom-call | tf_op jit(solution)/shard_map/jit(cholesky)/cholesky | solution.py:101
  97.7 0.6 compare_reduce_fusion
  98.4 0.7 fusion.41
  99.0 9.8 %custom-call.11 = f32[1,128,128]{1,2,0:T(8,128)S(1)} custom-call(f32[1,128,128]{2,1,0:T(8,128)S(1)} %fusion.41), custom_call_target="InvertDiagBlocksLowerTriangular" | custom-call | tf_op jit(solution)/shard_map/jit(_solve_triangular)/triangular_solve | solution.py:102
  108.9 0.3 fusion.28
  109.1 0.1 copy.49
  109.2 0.3 convolution_negate_fusion.1
  109.6 0.6 fusion.18
  110.2 0.4 convolution_negate_fusion
  110.5 3.6 %fusion = bf16[1024,512]{0,1:T(8,128)(2,1)S(1)} fusion(f32[1024,512]{1,0:T(8,128)S(1)} %bitcast.81, f32[256,256]{1,0:T(8,128)S(1)} %select_maximum_fusion.2, f32[128,128]{1,0:T(8,128)S(1)} %copy.49, f32[128,128]{1,0:T(8,128)S(1)} %convolution_negate_fusion.1, f32[128,256]{1,0:T(8,128)S(1)} %concatenate.40, f32[256,256]{1,0:T(8,128)S(1)} %convolution_negate_fusion), kind=kOutput, calls=%fused_computation.3 | convolution fusion | flops 3223322624 | bytes 3932160 | tf_op jit(solution)/shard_map/dot_general | solution.py:135
  114.1 0.0 copy-start.5
  114.1 0.0 copy-start.2
  114.1 1.3 copy.59
  115.5 0.0 all-gather.2.cloned.1.call-update
  115.5 0.0 reduce-scatter.2.cloned.1.call-start
  115.6 0.7 gather_fusion.1
  116.2 0.7 gather_fusion
  116.9 0.5 broadcast_maximum_fusion.1.left_ref
  117.4 0.5 broadcast_maximum_fusion.right_ref
  118.0 0.5 and_convert_fusion.live_ref
  118.5 112.5 %all-gather.2.cloned.1.call-done.refs_0_.refs_1_.refs_2_.refs_3_.refs_4_.refs_5_.refs_6_.refs_7_.refs_8_.refs_9_.refs_10_.refs_11_.refs_12_.refs_13_.refs_14_.refs_15_ = bf16[128,256,512]{2,1,0:T(8,128)(2,1)} async-done(((bf16[4,256,512]{2,1,0:T(8,128)(2,1)}), bf16[128,256,512]{2,1,0:T(8,128)(2,1)}) %all-gather.2.cloned.1.call-update) | async-done | bytes 33554448 | tf_op jit(solution)/shard_map/all_gather | solution.py:138
  231.0 6.2 %shard_map.95 = bf16[16,256,256]{2,1,0:T(8,128)(2,1)} custom-call(s32[16]{0:T(128)} %broadcast_maximum_fusion.1.left_ref, s32[16]{0:T(128)} %broadcast_maximum_fusion.right_ref, s32[16]{0:T(128)} %and_convert_fusion.live_ref, ...), custom_call_target="tpu_custom_call" | custom-call | flops 1073741824 | bytes 12582912 | tf_op jit(solution)/shard_map/pallas_call | solution.py:73
  237.2 0.0 reduce-scatter.2.cloned.1.call-update
  237.2 0.7 copy-done.6
  237.9 0.6 fusion.54.live_ref
  238.4 0.6 maximum_bitcast_fusion
  239.0 23.7 %shard_map.94 = bf16[80,256,256]{2,1,0:T(8,128)(2,1)} custom-call(s32[80]{0:T(128)} %get-tuple-element.21.left_ref, s32[80]{0:T(128)} %get-tuple-element.20.right_ref, s32[80]{0:T(128)} %fusion.54.live_ref, ...), custom_call_target="tpu_custom_call" | custom-call | flops 5368709120 | bytes 62914560 | tf_op jit(solution)/shard_map/pallas_call | solution.py:73
  262.8 4.3 %reduce-scatter.2.cloned.1.call-done = bf16[4,256,256]{2,1,0:T(8,128)(2,1)} async-done(((bf16[16,256,256]{2,1,0:T(8,128)(2,1)}), bf16[4,256,256]{2,1,0:T(8,128)(2,1)}) %reduce-scatter.2.cloned.1.call-update) | async-done | bytes 524304 | tf_op jit(solution)/shard_map/reduce_scatter | solution.py:165
  267.1 2.0 fusion.10
  (23 shorter events, 0.3 us)
Async XLA Ops:
  7.2 103.4 %copy-start = (f32[1,4,256,512]{3,2,1,0:T(8,128)S(1)}, f32[1,4,256,512]{3,2,1,0:T(8,128)}, u32[]{:S(2)}) copy-start(f32[1,4,256,512]{3,2,1,0:T(8,128)} %param.11) | copy-start | bytes 6291460
  7.2 223.8 %all-gather.2.cloned.1.call-start = ((), (), s32[]{:S(2)}) async-start(), calls=%async_computation.1 | async-start | bytes 34603008 | tf_op jit(solution)/shard_map/all_gather | solution.py:138
  33.2 0.8 copy-start.3
  114.1 1.4 copy-start.5
  114.1 1.4 copy-start.2
  115.5 151.6 %reduce-scatter.2.cloned.1.call-start = ((), (), s32[]{:S(2)}) async-start(), calls=%async_computation.2 | async-start | bytes 2621440 | tf_op jit(solution)/shard_map/reduce_scatter | solution.py:165
  237.2 0.7 copy-start.6
  239.0 28.0 %copy-start.4 = (bf16[1,4,256,256]{3,2,1,0:T(8,128)(2,1)S(1)}, bf16[1,4,256,256]{3,2,1,0:T(8,128)(2,1)}, u32[]{:S(2)}) copy-start(bf16[1,4,256,256]{3,2,1,0:T(8,128)(2,1)} %param.14) | copy-start | bytes 1572868
  239.0 30.0 %copy-start.1 = (f32[1,4,256,512]{3,2,1,0:T(8,128)S(1)}, f32[1,4,256,512]{3,2,1,0:T(8,128)}, u32[]{:S(2)}) copy-start(f32[1,4,256,512]{3,2,1,0:T(8,128)} %param.11) | copy-start | bytes 6291460
Sparse Core Ops, SparseCore 0:
  115.6 115.3 all-gather.1
  237.3 29.6 reduce-scatter.1
where the time goes:
time: 279 us; the launch traced here: 276 us
  waiting for transfers between devices  117 us (42%)
  other arithmetic  97.3 us (35%)
  Pallas kernels  29.9 us (11%)
  between operations  14.4 us (5%)
  matrix products  10.8 us (4%)
  local copies, waits for them, and re-layouts  6.44 us (2%)
    all_gather x1, waiting for transfers between devices, on_device(): rows_all = lax.all_gather(panel_here, 'blk', axis=0, tiled=True)  112 us
    another operation x12, other arithmetic, _inverse_factor(): l_kk = jnp.linalg.cholesky(head)  49.8 us
    another operation x8, other arithmetic, _inverse_factor(): inv_kk = jax.scipy.linalg.solve_triangular(l_kk, eye, lower=True)  42 us
    pallas_call x2, Pallas kernels, pair_products(): pl.pallas_call(functools.partial(_pair_kernel, k, targets is not None), g...  29.9 us
    dot_general x12, matrix products, _dot(): return jnp.dot(a, b, precision=lax.Precision.HIGHEST)  6.15 us
  transfers between devices with their start and end apart: 2, of which 2 were waited for; matrix products, arithmetic and copies ran while one was open for 1% of the time, Pallas kernels for 9%

commit v1 on v0

--- a/solution.py
+++ b/solution.py
@@ -47,6 +47,8 @@
     count = left.shape[0]
     _, width, depth = rows_all.shape
     steps = count // k
+    left = _held(left, live, k)
+    right = _held(right, live, k)
 
     def row_map(j, which):
         def index(i, l_ref, r_ref, v_ref):
@@ -77,6 +79,15 @@
         compiler_params=pltpu.CompilerParams(dimension_semantics=("arbitrary",)),
         cost_estimate=pl.CostEstimate(flops=flops, bytes_accessed=bytes_accessed, transcendentals=0),
     )(left, right, live, *operands)
+
+
+def _held(index, live, k):
+    index = index.reshape(-1, k)
+    keep = live.reshape(-1, k) > 0
+    rows = [index[0]]
+    for i in range(1, index.shape[0]):
+        rows.append(jnp.where(keep[i], index[i], rows[-1]))
+    return jnp.stack(rows).reshape(-1)
 
 
 def _step_of(count, limit=4):

time: 279 us -> 278 us (level)
  waiting for transfers between devices: 117 us -> 112 us
  Pallas kernels: 29.9 us -> 34.4 us
    pallas_call x2, Pallas kernels: 29.9 us -> 34.4 us  [pair_products(): pl.pallas_call(functools.partial(_pair_kernel, k, targets is not None), g...]
    reduce_scatter x1, waiting for transfers between devices: 4.3 us -> 0.02 us  [on_device(): lax.psum_scatter(partial, 'leaf', scatter_dimension=0, tiled=True)]
  transfers between devices with their start and end apart: 2 -> 2, of which waited for: 2 -> 1; matrix products, arithmetic and copies ran while one was open for 1% -> 2% of each run, Pallas kernels for 9% -> 10%
where the time goes in v1:
time: 278 us; the launch traced here: 277 us
  waiting for transfers between devices  112 us (40%)
  other arithmetic  95.9 us (34%)
  Pallas kernels  34.4 us (12%)
  between operations  14.5 us (5%)
  matrix products  10.8 us (4%)
  local copies, waits for them, and re-layouts  9.08 us (3%)
    all_gather x1, waiting for transfers between devices, on_device(): rows_all = lax.all_gather(panel_here, 'blk', axis=0, tiled=True)  112 us
    another operation x12, other arithmetic, _inverse_factor(): l_kk = jnp.linalg.cholesky(head)  49.8 us
    another operation x8, other arithmetic, _inverse_factor(): inv_kk = jax.scipy.linalg.solve_triangular(l_kk, eye, lower=True)  42 us
    pallas_call x2, Pallas kernels, pair_products(): pl.pallas_call(functools.partial(_pair_kernel, k, targets is not None), g...  34.4 us
    dot_general x12, matrix products, _dot(): return jnp.dot(a, b, precision=lax.Precision.HIGHEST)  6.15 us
  transfers between devices with their start and end apart: 2, of which 1 were waited for; matrix products, arithmetic and copies ran while one was open for 2% of the time, Pallas kernels for 10%

profile of v1, /device:TPU:33, one launch (start us, length us, event | category | flops | bytes accessed | tf_op | source)
XLA Modules:
  0.0 277.0 jit_solution(1100844508894986705)
XLA Ops:
  7.2 0.0 all-gather.2.cloned.1.call-start
  7.2 1.7 copy.38
  8.9 0.1 copy.39
  9.1 11.7 %cholesky.74 = f32[128,128]{1,0:T(8,128)S(1)} custom-call(f32[128,128]{1,0:T(8,128)S(1)} %fusion.53), custom_call_target="Cholesky" | custom-call | tf_op jit(solution)/shard_map/jit(cholesky)/cholesky | solution.py:112
  20.8 0.6 compare_reduce_fusion.3
  21.5 0.7 fusion.38
  22.1 9.8 %custom-call.8 = f32[1,128,128]{1,2,0:T(8,128)S(1)} custom-call(f32[1,128,128]{2,1,0:T(8,128)S(1)} %fusion.38), custom_call_target="InvertDiagBlocksLowerTriangular" | custom-call | tf_op jit(solution)/shard_map/jit(_solve_triangular)/triangular_solve | solution.py:113
  31.9 0.3 fusion.34
  32.2 0.3 fusion.26
  32.5 0.7 convolution_subtract_fusion
  33.2 0.8 copy-done.3
  34.1 0.1 copy.41
  34.2 0.9 fusion.51
  35.0 11.7 %cholesky.85 = f32[128,128]{1,0:T(8,128)S(1)} custom-call(f32[128,128]{1,0:T(8,128)S(1)} %fusion.51), custom_call_target="Cholesky" | custom-call | tf_op jit(solution)/shard_map/jit(cholesky)/cholesky | solution.py:112
  46.8 0.6 compare_reduce_fusion.2
  47.4 0.7 fusion.39
  48.1 9.9 %custom-call.9 = f32[1,128,128]{1,2,0:T(8,128)S(1)} custom-call(f32[1,128,128]{2,1,0:T(8,128)S(1)} %fusion.39), custom_call_target="InvertDiagBlocksLowerTriangular" | custom-call | tf_op jit(solution)/shard_map/jit(_solve_triangular)/triangular_solve | solution.py:113
  58.0 0.3 fusion.32
  58.3 0.1 copy.43
  58.4 1.2 fusion.36
  59.6 0.3 fusion.44
  59.9 1.4 convolution_subtract_fusion.1
  61.3 0.1 copy.45
  61.4 11.7 %cholesky.96 = f32[128,128]{1,0:T(8,128)S(1)} custom-call(f32[128,128]{1,0:T(8,128)S(1)} %fusion.49), custom_call_target="Cholesky" | custom-call | tf_op jit(solution)/shard_map/jit(cholesky)/cholesky | solution.py:112
  73.2 0.6 compare_reduce_fusion.1
  73.8 0.7 fusion.40
  74.5 9.8 %custom-call.10 = f32[1,128,128]{1,2,0:T(8,128)S(1)} custom-call(f32[1,128,128]{2,1,0:T(8,128)S(1)} %fusion.40), custom_call_target="InvertDiagBlocksLowerTriangular" | custom-call | tf_op jit(solution)/shard_map/jit(_solve_triangular)/triangular_solve | solution.py:113
  84.3 0.3 fusion.30
  84.6 0.3 fusion.42
  84.9 0.3 convolution_subtract_fusion.2
  85.1 0.2 fusion.63
  85.4 0.3 convolution_negate_fusion.2
  85.7 0.1 copy.47
  85.8 11.9 %cholesky.107 = f32[128,128]{1,0:T(8,128)S(1)} custom-call(f32[128,128]{1,0:T(8,128)S(1)} %fusion.47), custom_call_target="Cholesky" | custom-call | tf_op jit(solution)/shard_map/jit(cholesky)/cholesky | solution.py:112
  97.7 0.6 compare_reduce_fusion
  98.4 0.7 fusion.41
  99.0 9.8 %custom-call.11 = f32[1,128,128]{1,2,0:T(8,128)S(1)} custom-call(f32[1,128,128]{2,1,0:T(8,128)S(1)} %fusion.41), custom_call_target="InvertDiagBlocksLowerTriangular" | custom-call | tf_op jit(solution)/shard_map/jit(_solve_triangular)/triangular_solve | solution.py:113
  108.9 0.3 fusion.28
  109.1 0.1 copy.49
  109.2 0.3 convolution_negate_fusion.1
  109.6 0.6 fusion.18
  110.2 0.4 convolution_negate_fusion
  110.5 3.6 %fusion = bf16[1024,512]{0,1:T(8,128)(2,1)S(1)} fusion(f32[1024,512]{1,0:T(8,128)S(1)} %bitcast.221, f32[256,256]{1,0:T(8,128)S(1)} %select_maximum_fusion.2, f32[128,128]{1,0:T(8,128)S(1)} %copy.49, f32[128,128]{1,0:T(8,128)S(1)} %convolution_negate_fusion.1, f32[128,256]{1,0:T(8,128)S(1)} %concatenate.40, f32[256,256]{1,0:T(8,128)S(1)} %convolution_negate_fusion), kind=kOutput, calls=%fused_computation.3 | convolution fusion | flops 3223322624 | bytes 3932160 | tf_op jit(solution)/shard_map/dot_general | solution.py:146
  114.1 1.3 copy.59
  115.5 0.0 all-gather.2.cloned.1.call-update
  115.5 0.0 reduce-scatter.2.cloned.1.call-start
  115.6 0.7 gather_fusion.1
  116.2 0.7 gather_fusion
  116.9 0.5 broadcast_compare_fusion
  117.5 0.1 bitcast_select_fusion
  117.6 0.6 reshape.310.right_ref
  118.2 0.6 reshape.309.left_ref
  118.8 112.2 %all-gather.2.cloned.1.call-done.refs_0_.refs_1_.refs_2_.refs_3_.refs_4_.refs_5_.refs_6_.refs_7_.refs_8_.refs_9_.refs_10_.refs_11_.refs_12_.refs_13_.refs_14_.refs_15_ = bf16[128,256,512]{2,1,0:T(8,128)(2,1)} async-done(((bf16[4,256,512]{2,1,0:T(8,128)(2,1)}), bf16[128,256,512]{2,1,0:T(8,128)(2,1)}) %all-gather.2.cloned.1.call-update) | async-done | bytes 33554448 | tf_op jit(solution)/shard_map/all_gather | solution.py:149
  231.0 5.7 %shard_map.95 = bf16[16,256,256]{2,1,0:T(8,128)(2,1)} custom-call(s32[16]{0:T(128)} %reshape.309.left_ref, s32[16]{0:T(128)} %reshape.310.right_ref, s32[16]{0:T(128)} %get-tuple-element.21.live_ref, ...), custom_call_target="tpu_custom_call" | custom-call | flops 1073741824 | bytes 12582912 | tf_op jit(solution)/shard_map/pallas_call | solution.py:75
  236.7 0.0 reduce-scatter.2.cloned.1.call-update
  236.7 0.7 copy-done.6
  237.4 0.5 fusion.54
  237.9 0.1 bitcast_select_fusion.6
  238.1 0.7 reshape.308.right_ref
  238.7 0.1 bitcast_select_fusion.7
  238.9 0.7 reshape.307.left_ref
  239.5 28.6 %shard_map.94 = bf16[80,256,256]{2,1,0:T(8,128)(2,1)} custom-call(s32[80]{0:T(128)} %reshape.307.left_ref, s32[80]{0:T(128)} %reshape.308.right_ref, s32[80]{0:T(128)} %get-tuple-element.46.live_ref, ...), custom_call_target="tpu_custom_call" | custom-call | flops 5368709120 | bytes 62914560 | tf_op jit(solution)/shard_map/pallas_call | solution.py:75
  268.2 0.0 reduce-scatter.2.cloned.1.call-done
  268.2 2.0 fusion.10
  (37 shorter events, 0.5 us)
Async XLA Ops:
  7.2 103.4 %copy-start = (f32[1,4,256,512]{3,2,1,0:T(8,128)S(1)}, f32[1,4,256,512]{3,2,1,0:T(8,128)}, u32[]{:S(2)}) copy-start(f32[1,4,256,512]{3,2,1,0:T(8,128)} %param.11) | copy-start | bytes 6291460
  7.2 223.8 %all-gather.2.cloned.1.call-start = ((), (), s32[]{:S(2)}) async-start(), calls=%async_computation.1 | async-start | bytes 34603008 | tf_op jit(solution)/shard_map/all_gather | solution.py:149
  33.2 0.8 copy-start.3
  114.1 1.4 copy-start.5
  114.1 1.4 copy-start.2
  115.5 152.7 %reduce-scatter.2.cloned.1.call-start = ((), (), s32[]{:S(2)}) async-start(), calls=%async_computation.2 | async-start | bytes 2621440 | tf_op jit(solution)/shard_map/reduce_scatter | solution.py:176
  236.7 0.7 copy-start.6
  239.5 28.7 %copy-start.4 = (bf16[1,4,256,256]{3,2,1,0:T(8,128)(2,1)S(1)}, bf16[1,4,256,256]{3,2,1,0:T(8,128)(2,1)}, u32[]{:S(2)}) copy-start(bf16[1,4,256,256]{3,2,1,0:T(8,128)(2,1)} %param.14) | copy-start | bytes 1572868
  239.5 30.6 %copy-start.1 = (f32[1,4,256,512]{3,2,1,0:T(8,128)S(1)}, f32[1,4,256,512]{3,2,1,0:T(8,128)}, u32[]{:S(2)}) copy-start(f32[1,4,256,512]{3,2,1,0:T(8,128)} %param.11) | copy-start | bytes 6291460
Sparse Core Ops, SparseCore 0:
  115.6 115.3 all-gather.1
  236.9 29.6 reduce-scatter.1

commit v2 on v1

--- a/solution.py
+++ b/solution.py
@@ -143,7 +143,7 @@
     count, width, depth = rows_local.shape
     inverse = _inverse_factor(diagonal, 128)
     flat = rows_local.reshape(count * width, depth)
-    joined = jnp.dot(flat, inverse.T, precision=lax.Precision.HIGHEST)
+    joined = jnp.dot(flat, inverse.T, precision=lax.Precision.HIGH)
     panel_here = joined.reshape(count, width, depth).astype(jnp.bfloat16)
 
     rows_all = lax.all_gather(panel_here, "blk", axis=0, tiled=True)

time: 278 us -> 279 us (level); the launches traced: 277 us -> 274 us
  Pallas kernels: 34.4 us -> 22.9 us
  waiting for transfers between devices: 112 us -> 123 us
    pallas_call x2, Pallas kernels: 34.4 us -> 22.9 us  [pair_products(): pl.pallas_call(functools.partial(_pair_kernel, k, targets is not None), g...]
    reduce_scatter x1, waiting for transfers between devices: 0.02 us -> 10.5 us  [on_device(): lax.psum_scatter(partial, 'leaf', scatter_dimension=0, tiled=True)]
  transfers between devices with their start and end apart: 2 -> 2, of which waited for: 1 -> 2; matrix products, arithmetic and copies ran while one was open for 2% -> 2% of each run, Pallas kernels for 10% -> 6%
where the time goes in v2:
time: 279 us; the launch traced here: 274 us
  waiting for transfers between devices  123 us (44%)
  other arithmetic  95.9 us (34%)
  Pallas kernels  22.9 us (8%)
  between operations  14.5 us (5%)
  matrix products  9.1 us (3%)
  local copies, waits for them, and re-layouts  9.08 us (3%)
    all_gather x1, waiting for transfers between devices, on_device(): rows_all = lax.all_gather(panel_here, 'blk', axis=0, tiled=True)  112 us
    another operation x12, other arithmetic, _inverse_factor(): l_kk = jnp.linalg.cholesky(head)  49.8 us
    another operation x8, other arithmetic, _inverse_factor(): inv_kk = jax.scipy.linalg.solve_triangular(l_kk, eye, lower=True)  42 us
    pallas_call x2, Pallas kernels, pair_products(): pl.pallas_call(functools.partial(_pair_kernel, k, targets is not None), g...  22.9 us
    reduce_scatter x1, waiting for transfers between devices, on_device(): lax.psum_scatter(partial, 'leaf', scatter_dimension=0, tiled=True)  10.5 us
    dot_general x12, matrix products, _dot(): return jnp.dot(a, b, precision=lax.Precision.HIGHEST)  6.15 us
  transfers between devices with their start and end apart: 2, of which 2 were waited for; matrix products, arithmetic and copies ran while one was open for 2% of the time, Pallas kernels for 6%

profile of v2, /device:TPU:33, one launch (start us, length us, event | category | flops | bytes accessed | tf_op | source)
XLA Modules:
  0.0 274.3 jit_solution(6494129729544438267)
XLA Ops:
  7.2 0.0 all-gather.2.cloned.1.call-start
  7.2 1.7 copy.38
  8.9 0.1 copy.39
  9.1 11.7 %cholesky.74 = f32[128,128]{1,0:T(8,128)S(1)} custom-call(f32[128,128]{1,0:T(8,128)S(1)} %fusion.53), custom_call_target="Cholesky" | custom-call | tf_op jit(solution)/shard_map/jit(cholesky)/cholesky | solution.py:112
  20.8 0.6 compare_reduce_fusion.3
  21.5 0.7 fusion.38
  22.1 9.8 %custom-call.8 = f32[1,128,128]{1,2,0:T(8,128)S(1)} custom-call(f32[1,128,128]{2,1,0:T(8,128)S(1)} %fusion.38), custom_call_target="InvertDiagBlocksLowerTriangular" | custom-call | tf_op jit(solution)/shard_map/jit(_solve_triangular)/triangular_solve | solution.py:113
  31.9 0.3 fusion.34
  32.2 0.3 fusion.26
  32.5 0.7 convolution_subtract_fusion
  33.2 0.8 copy-done.3
  34.1 0.1 copy.41
  34.2 0.9 fusion.51
  35.0 11.7 %cholesky.85 = f32[128,128]{1,0:T(8,128)S(1)} custom-call(f32[128,128]{1,0:T(8,128)S(1)} %fusion.51), custom_call_target="Cholesky" | custom-call | tf_op jit(solution)/shard_map/jit(cholesky)/cholesky | solution.py:112
  46.8 0.6 compare_reduce_fusion.2
  47.4 0.7 fusion.39
  48.1 9.9 %custom-call.9 = f32[1,128,128]{1,2,0:T(8,128)S(1)} custom-call(f32[1,128,128]{2,1,0:T(8,128)S(1)} %fusion.39), custom_call_target="InvertDiagBlocksLowerTriangular" | custom-call | tf_op jit(solution)/shard_map/jit(_solve_triangular)/triangular_solve | solution.py:113
  58.0 0.3 fusion.32
  58.3 0.1 copy.43
  58.4 1.2 fusion.36
  59.6 0.3 fusion.44
  59.9 1.4 convolution_subtract_fusion.1
  61.3 0.1 copy.45
  61.4 11.7 %cholesky.96 = f32[128,128]{1,0:T(8,128)S(1)} custom-call(f32[128,128]{1,0:T(8,128)S(1)} %fusion.49), custom_call_target="Cholesky" | custom-call | tf_op jit(solution)/shard_map/jit(cholesky)/cholesky | solution.py:112
  73.2 0.6 compare_reduce_fusion.1
  73.8 0.7 fusion.40
  74.5 9.8 %custom-call.10 = f32[1,128,128]{1,2,0:T(8,128)S(1)} custom-call(f32[1,128,128]{2,1,0:T(8,128)S(1)} %fusion.40), custom_call_target="InvertDiagBlocksLowerTriangular" | custom-call | tf_op jit(solution)/shard_map/jit(_solve_triangular)/triangular_solve | solution.py:113
  84.3 0.3 fusion.30
  84.6 0.3 fusion.42
  84.9 0.3 convolution_subtract_fusion.2
  85.1 0.2 fusion.63
  85.4 0.3 convolution_negate_fusion.2
  85.7 0.1 copy.47
  85.8 11.9 %cholesky.107 = f32[128,128]{1,0:T(8,128)S(1)} custom-call(f32[128,128]{1,0:T(8,128)S(1)} %fusion.47), custom_call_target="Cholesky" | custom-call | tf_op jit(solution)/shard_map/jit(cholesky)/cholesky | solution.py:112
  97.7 0.6 compare_reduce_fusion
  98.4 0.7 fusion.41
  99.0 9.8 %custom-call.11 = f32[1,128,128]{1,2,0:T(8,128)S(1)} custom-call(f32[1,128,128]{2,1,0:T(8,128)S(1)} %fusion.41), custom_call_target="InvertDiagBlocksLowerTriangular" | custom-call | tf_op jit(solution)/shard_map/jit(_solve_triangular)/triangular_solve | solution.py:113
  108.9 0.3 fusion.28
  109.1 0.1 copy.49
  109.2 0.3 convolution_negate_fusion.1
  109.6 0.6 fusion.18
  110.2 0.4 convolution_negate_fusion
  110.5 1.8 fusion
  112.4 1.3 copy.59
  113.8 0.0 all-gather.2.cloned.1.call-update
  113.8 0.0 reduce-scatter.2.cloned.1.call-start
  113.9 0.7 gather_fusion.1
  114.5 0.7 gather_fusion
  115.2 0.5 broadcast_compare_fusion
  115.7 0.1 bitcast_select_fusion
  115.8 0.6 reshape.310.right_ref
  116.5 0.6 reshape.309.left_ref
  117.1 112.2 %all-gather.2.cloned.1.call-done.refs_0_.refs_1_.refs_2_.refs_3_.refs_4_.refs_5_.refs_6_.refs_7_.refs_8_.refs_9_.refs_10_.refs_11_.refs_12_.refs_13_.refs_14_.refs_15_ = bf16[128,256,512]{2,1,0:T(8,128)(2,1)} async-done(((bf16[4,256,512]{2,1,0:T(8,128)(2,1)}), bf16[128,256,512]{2,1,0:T(8,128)(2,1)}) %all-gather.2.cloned.1.call-update) | async-done | bytes 33554448 | tf_op jit(solution)/shard_map/all_gather | solution.py:149
  229.3 5.7 %shard_map.95 = bf16[16,256,256]{2,1,0:T(8,128)(2,1)} custom-call(s32[16]{0:T(128)} %reshape.309.left_ref, s32[16]{0:T(128)} %reshape.310.right_ref, s32[16]{0:T(128)} %get-tuple-element.21.live_ref, ...), custom_call_target="tpu_custom_call" | custom-call | flops 1073741824 | bytes 12582912 | tf_op jit(solution)/shard_map/pallas_call | solution.py:75
  235.0 0.0 reduce-scatter.2.cloned.1.call-update
  235.0 0.7 copy-done.6
  235.7 0.5 fusion.54
  236.2 0.1 bitcast_select_fusion.6
  236.3 0.7 reshape.308.right_ref
  237.0 0.1 bitcast_select_fusion.7
  237.1 0.7 reshape.307.left_ref
  237.8 17.2 %shard_map.94 = bf16[80,256,256]{2,1,0:T(8,128)(2,1)} custom-call(s32[80]{0:T(128)} %reshape.307.left_ref, s32[80]{0:T(128)} %reshape.308.right_ref, s32[80]{0:T(128)} %get-tuple-element.46.live_ref, ...), custom_call_target="tpu_custom_call" | custom-call | flops 5368709120 | bytes 62914560 | tf_op jit(solution)/shard_map/pallas_call | solution.py:75
  255.0 10.5 %reduce-scatter.2.cloned.1.call-done = bf16[4,256,256]{2,1,0:T(8,128)(2,1)} async-done(((bf16[16,256,256]{2,1,0:T(8,128)(2,1)}), bf16[4,256,256]{2,1,0:T(8,128)(2,1)}) %reduce-scatter.2.cloned.1.call-update) | async-done | bytes 524304 | tf_op jit(solution)/shard_map/reduce_scatter | solution.py:176
  265.5 2.0 fusion.10
  (37 shorter events, 0.5 us)
Async XLA Ops:
  7.2 103.4 %copy-start = (f32[1,4,256,512]{3,2,1,0:T(8,128)S(1)}, f32[1,4,256,512]{3,2,1,0:T(8,128)}, u32[]{:S(2)}) copy-start(f32[1,4,256,512]{3,2,1,0:T(8,128)} %param.11) | copy-start | bytes 6291460
  7.2 222.1 %all-gather.2.cloned.1.call-start = ((), (), s32[]{:S(2)}) async-start(), calls=%async_computation.1 | async-start | bytes 34603008 | tf_op jit(solution)/shard_map/all_gather | solution.py:149
  33.2 0.8 copy-start.3
  112.4 1.4 copy-start.5
  112.4 1.4 copy-start.2
  113.8 151.7 %reduce-scatter.2.cloned.1.call-start = ((), (), s32[]{:S(2)}) async-start(), calls=%async_computation.2 | async-start | bytes 2621440 | tf_op jit(solution)/shard_map/reduce_scatter | solution.py:176
  235.0 0.7 copy-start.6
  237.8 27.7 %copy-start.4 = (bf16[1,4,256,256]{3,2,1,0:T(8,128)(2,1)S(1)}, bf16[1,4,256,256]{3,2,1,0:T(8,128)(2,1)}, u32[]{:S(2)}) copy-start(bf16[1,4,256,256]{3,2,1,0:T(8,128)(2,1)} %param.14) | copy-start | bytes 1572868
  237.8 29.6 %copy-start.1 = (f32[1,4,256,512]{3,2,1,0:T(8,128)S(1)}, f32[1,4,256,512]{3,2,1,0:T(8,128)}, u32[]{:S(2)}) copy-start(f32[1,4,256,512]{3,2,1,0:T(8,128)} %param.11) | copy-start | bytes 6291460
Sparse Core Ops, SparseCore 0:
  113.9 115.3 all-gather.1
  235.1 30.2 reduce-scatter.1
